TPU v7x, 512 devices: a whole 4x8x8 slice. The times are simulated.
512 devices in a mesh: section: 2 (over z_lo), tensor: 4 (over x), seq: 64 (over y, z_hi, core).
Axes of the slice: x: 4, y: 8, z: 8 (z_hi: 4, z_lo: 2; z = z_hi * 2 + z_lo), core: 2. Of those that a mesh axis runs over, the one named last changes fastest.
Arguments:
- tokens: bfloat16 [16384, 2560], P('seq', ('section', 'tensor')), may hold values from -6 to 6
- w_query: bfloat16 [2560, 2048], P(None, ('section', 'tensor')), may hold values from -0.125 to 0.125
- w_keyval: bfloat16 [2560, 2048], P(None, ('section', 'tensor')), may hold values from -0.125 to 0.125
- w_out: bfloat16 [2048, 2560], P(('section', 'tensor')), may hold values from -0.125 to 0.125
- w_gateup: bfloat16 [2560, 2, 5120], P('seq', None, ('section', 'tensor')), may hold values from -0.125 to 0.125
- attn_gain: float32 [2560], replicated, may hold values from 0.1 to 1.9
- post_gain: float32 [2560], replicated, may hold values from 0.1 to 1.9
- mlp_gain: float32 [2560], replicated, may hold values from 0.1 to 1.9
- query_gain: float32 [256], replicated, may hold values from 0.7 to 6.5
- key_gain: float32 [256], replicated, may hold values from 0.7 to 6.5
- prompt_lengths: int32 [8], replicated, may hold values from 1 to 4096, as said below
- page_slots: int32 [128], P('seq'), may hold values from 0 to 1, as said below
Outputs:
- hidden: bfloat16 [16384, 5120], P('seq', ('section', 'tensor'))
- page_cache: bfloat16 [128, 128, 2048], P('seq', None, ('section', 'tensor'))
Inputs may be any that keep to these rules, and one draw needn't show every extreme that they name: `prompt_lengths`: each prompt has at least one token; they sum to 16384; one prompt has exactly 4096 tokens and begins strictly inside a token block. `page_slots`: within each aligned group of 2 pages (the pages of one token block) the slots are a permutation of 0 to 1.
All inputs are finite; a program needn't handle non-finite values.
Results may differ from a plain program's by a relative error of at most 0.01.
The roundings to bfloat16 on the way count: a program that leaves them out, or rounds other values in their place, can miss the bound.
Values may be sent and summed in bfloat16 or wider, within the bound.
No kernel may reach another device: no remote copies, remote signals or barrier semaphores. Data moves between devices by JAX's collectives and lax.ppermute only.
A program may use at most 64 MiB of HBM per device.

v0:
```python
import jax
import jax.numpy as jnp
from jax import lax
from jax.sharding import PartitionSpec as P

REACH = 16
NORM_EPS = 1e-06
ROPE_BASE = 1000000.0
ROPE_FACTOR = 8.0


def swapped(value, axis, bit):
    mask = 2**bit
    pairs = [(source, source ^ mask) for source in range(lax.axis_size(axis))]
    return lax.ppermute(value, axis, pairs)


def shifted(block, axis, distance):
    devices = range(lax.axis_size(axis))
    route = [(i - distance, i) for i in devices if i - distance in devices]
    return lax.ppermute(block, axis, route)


def rms_norm(values, weights):
    values = values.astype(jnp.float32)
    inverse = lax.rsqrt(jnp.mean(values * values, axis=-1, keepdims=True) + NORM_EPS)
    return values * inverse * weights


def angle_tables(position, head_width):
    halfway = head_width // 2
    exponent = jnp.arange(halfway, dtype=jnp.float32) * (2.0 / head_width)
    frequency = ROPE_BASE ** (-exponent)
    angles = (position.astype(jnp.float32) / ROPE_FACTOR)[:, None] * frequency[None, :]
    return (jnp.cos(angles), jnp.sin(angles))


def rotary(values, cosine_table, sine_table):
    halfway = values.shape[-1] // 2
    lower_half = values[..., :halfway]
    upper_half = values[..., halfway:]
    return jnp.concatenate(
        [
            lower_half * cosine_table - upper_half * sine_table,
            upper_half * cosine_table + lower_half * sine_table,
        ],
        axis=-1,
    )


def local(
    tokens,
    w_query,
    w_keyval,
    w_out,
    w_gateup,
    attn_gain,
    post_gain,
    mlp_gain,
    query_gain,
    key_gain,
    prompt_lengths,
    page_slots,
):
    row_count = tokens.shape[0]
    head_width = w_query.shape[1]
    halfway = head_width // 2
    unit_count = w_gateup.shape[2]
    span_blocks = min(REACH, lax.axis_size("seq") // 2)
    features = lax.all_gather(tokens, ("section", "tensor"), axis=1, tiled=True)
    first_row = lax.axis_index("seq") * row_count
    prompt_ends = jnp.cumsum(prompt_lengths)
    prompt_starts = prompt_ends - prompt_lengths
    query_index = first_row + jnp.arange(row_count, dtype=jnp.int32)
    query_segment = jnp.sum(
        (prompt_ends[None, :] <= query_index[:, None]).astype(jnp.int32), axis=1
    )
    chosen = query_segment[:, None] == jnp.arange(prompt_ends.shape[0], dtype=jnp.int32)[None, :]
    query_position = query_index - jnp.sum(jnp.where(chosen, prompt_starts[None, :], 0), axis=1)
    cosine_table, sine_table = angle_tables(query_position, head_width)
    normed = rms_norm(features, attn_gain).astype(jnp.bfloat16)
    queries = jnp.dot(normed, w_query, preferred_element_type=jnp.float32)
    queries = rotary(rms_norm(queries, query_gain), cosine_table, sine_table).astype(jnp.bfloat16)
    own_half = jnp.dot(normed, w_keyval, preferred_element_type=jnp.float32).astype(jnp.bfloat16)
    other_half = swapped(own_half, "tensor", 0)
    is_lower = lax.axis_index("tensor") % 2 == 0
    lower_part = jnp.where(is_lower, own_half, other_half)
    upper_part = jnp.where(is_lower, other_half, own_half)
    raw_keys = jnp.concatenate([lower_part[:, :halfway], upper_part[:, :halfway]], axis=1)
    values_full = jnp.concatenate([lower_part[:, halfway:], upper_part[:, halfway:]], axis=1)
    keys_full = rotary(rms_norm(raw_keys, key_gain), cosine_table, sine_table).astype(jnp.bfloat16)
    own_keys = jnp.where(is_lower, keys_full[:, :halfway], keys_full[:, halfway:])
    page_rows = jnp.concatenate([own_keys, own_half[:, halfway:]], axis=1)
    pages_here = page_slots.shape[0]
    page_rows = page_rows.reshape(pages_here, row_count // pages_here, head_width)
    page_cache = jnp.zeros_like(page_rows).at[page_slots].set(page_rows)
    key_block = jnp.stack([keys_full, values_full])
    received = [key_block]
    for distance in range(1, span_blocks + 1):
        received.append(shifted(key_block, "seq", distance))
    window_stack = jnp.stack(received)
    all_keys = window_stack[:, 0].reshape(-1, head_width)
    all_values = window_stack[:, 1].reshape(-1, head_width)
    offsets = (jnp.arange(span_blocks + 1, dtype=jnp.int32) * row_count)[:, None]
    key_index = (first_row - offsets + jnp.arange(row_count, dtype=jnp.int32)[None, :]).reshape(-1)
    key_segment = jnp.sum((prompt_ends[None, :] <= key_index[:, None]).astype(jnp.int32), axis=1)
    key_segment = jnp.where(key_index >= 0, key_segment, -1)
    allowed = (key_segment[None, :] == query_segment[:, None]) & (
        key_index[None, :] <= query_index[:, None]
    )
    scores = lax.dot_general(
        queries, all_keys, (((1,), (1,)), ((), ())), preferred_element_type=jnp.float32
    ) * head_width ** (-0.5)
    scores = jnp.where(allowed, scores, -jnp.inf)
    row_max = jnp.max(scores, axis=1, keepdims=True)
    exponent_terms = jnp.exp(scores - row_max)
    weights_low = (exponent_terms / jnp.sum(exponent_terms, axis=1, keepdims=True)).astype(
        jnp.bfloat16
    )
    attention_out = jnp.dot(weights_low, all_values, preferred_element_type=jnp.float32).astype(
        jnp.bfloat16
    )
    head_terms = jnp.dot(attention_out, w_out, preferred_element_type=jnp.float32)
    attended = lax.psum(head_terms, ("section", "tensor"))
    residual = features.astype(jnp.float32) + rms_norm(attended, post_gain)
    ffn_input = rms_norm(residual, mlp_gain).astype(jnp.bfloat16)
    row_piece = lax.all_gather(w_gateup, "seq", axis=0, tiled=True)
    piece_rows = row_piece.shape[0]
    projected = jnp.dot(
        ffn_input, row_piece.reshape(piece_rows, 2 * unit_count), preferred_element_type=jnp.float32
    )
    hidden = (
        jax.nn.gelu(projected[:, :unit_count], approximate=True) * projected[:, unit_count:]
    ).astype(jnp.bfloat16)
    return (hidden, page_cache)


def solution(mesh):
    return jax.shard_map(
        local,
        mesh=mesh,
        in_specs=(
            P("seq", ("section", "tensor")),
            P(None, ("section", "tensor")),
            P(None, ("section", "tensor")),
            P(("section", "tensor"), None),
            P("seq", None, ("section", "tensor")),
            P(),
            P(),
            P(),
            P(),
            P(),
            P(),
            P("seq"),
        ),
        out_specs=(P("seq", ("section", "tensor")), P("seq", None, ("section", "tensor"))),
        check_vma=False,
    )
```

profile of v0, /device:TPU:8, one launch (start us, length us, event | category | flops | bytes accessed | tf_op | source)
XLA Modules:
  0.0 404.8 jit_solution(14164455643297318080)
XLA Ops:
  8.0 0.0 copy-start
  8.0 0.0 all-gather.3.cloned.1.call-start
  8.1 0.7 all-gather.3.cloned.1.call-update
  8.8 0.0 all-reduce.2.cloned.1.call-start
  8.8 0.8 reduce-window.8
  9.7 0.1 iota_add_fusion
  9.8 0.1 convert_reduce_fusion.1
  9.8 0.7 bitcast_subtract_fusion
  10.5 0.1 select_reduce_fusion
  10.6 0.1 convert_reduce_fusion
  10.7 49.9 %all-gather.3.cloned.1.call-done = bf16[256,2560]{0,1:T(8,128)(2,1)} async-done(((bf16[256,320]{0,1:T(8,128)(2,1)}), bf16[256,2560]{0,1:T(8,128)(2,1)}) %all-gather.3.cloned.1.call-update) | async-done | bytes 1310736 | tf_op jit(solution)/shard_map/all_gather | solution.py:70
  60.6 1.6 copy.24
  62.2 0.0 copy-start.8
  62.2 0.3 fusion.2
  62.6 2.1 convolution_convert_fusion
  64.7 0.0 copy-start.7
  64.7 1.9 collective-permute-start
  66.7 0.8 multiply_reduce_fusion.2
  67.5 0.1 multiply_multiply_fusion.1
  67.6 4.0 collective-permute-done
  71.6 0.1 fusion.25
  71.7 0.1 fusion.26
  71.8 0.6 broadcast_select_fusion.2
  72.5 1.9 collective-permute-start.1
  74.4 0.6 fusion.36
  75.0 4.6 %collective-permute-start.2 = (bf16[2,256,256]{1,2,0:T(8,128)(2,1)S(1)}, bf16[2,256,256]{1,2,0:T(8,128)(2,1)S(1)}, u32[]{:S(2)}, u32[]{:S(2)}) collective-permute-start(bf16[2,256,256]{1,2,0:T(8,128)(2,1)S(1)} %pad_maximum_fusion), channel_id=1, source_target_pairs={{0,2},{1,3},{2,4},{3,5},{4,6},{5,7},{6,8},{7,9},{8,10},{9,11},{10,... | collective-permute-start | bytes 786440 | tf_op jit(solution)/shard_map/ppermute | solution.py:21
  79.6 5.3 %collective-permute-start.3 = (bf16[2,256,256]{1,2,0:T(8,128)(2,1)S(1)}, bf16[2,256,256]{1,2,0:T(8,128)(2,1)S(1)}, u32[]{:S(2)}, u32[]{:S(2)}) collective-permute-start(bf16[2,256,256]{1,2,0:T(8,128)(2,1)S(1)} %pad_maximum_fusion), channel_id=1, source_target_pairs={{0,3},{1,4},{2,5},{3,6},{4,7},{5,8},{6,9},{7,10},{8,11},{9,12},{10... | collective-permute-start | bytes 786440 | tf_op jit(solution)/shard_map/ppermute | solution.py:21
  84.9 5.4 %collective-permute-start.4 = (bf16[2,256,256]{1,2,0:T(8,128)(2,1)S(1)}, bf16[2,256,256]{1,2,0:T(8,128)(2,1)S(1)}, u32[]{:S(2)}, u32[]{:S(2)}) collective-permute-start(bf16[2,256,256]{1,2,0:T(8,128)(2,1)S(1)} %pad_maximum_fusion), channel_id=1, source_target_pairs={{0,4},{1,5},{2,6},{3,7},{4,8},{5,9},{6,10},{7,11},{8,12},{9,13},{1... | collective-permute-start | bytes 786440 | tf_op jit(solution)/shard_map/ppermute | solution.py:21
  90.3 4.8 %collective-permute-start.5 = (bf16[2,256,256]{1,2,0:T(8,128)(2,1)S(1)}, bf16[2,256,256]{1,2,0:T(8,128)(2,1)S(1)}, u32[]{:S(2)}, u32[]{:S(2)}) collective-permute-start(bf16[2,256,256]{1,2,0:T(8,128)(2,1)S(1)} %pad_maximum_fusion), channel_id=1, source_target_pairs={{0,5},{1,6},{2,7},{3,8},{4,9},{5,10},{6,11},{7,12},{8,13},{9,14},{... | collective-permute-start | bytes 786440 | tf_op jit(solution)/shard_map/ppermute | solution.py:21
  95.1 6.0 %collective-permute-start.6 = (bf16[2,256,256]{1,2,0:T(8,128)(2,1)S(1)}, bf16[2,256,256]{1,2,0:T(8,128)(2,1)S(1)}, u32[]{:S(2)}, u32[]{:S(2)}) collective-permute-start(bf16[2,256,256]{1,2,0:T(8,128)(2,1)S(1)} %pad_maximum_fusion), channel_id=1, source_target_pairs={{0,6},{1,7},{2,8},{3,9},{4,10},{5,11},{6,12},{7,13},{8,14},{9,15},... | collective-permute-start | bytes 786440 | tf_op jit(solution)/shard_map/ppermute | solution.py:21
  101.2 18.7 %collective-permute-start.7 = (bf16[2,256,256]{1,2,0:T(8,128)(2,1)S(1)}, bf16[2,256,256]{1,2,0:T(8,128)(2,1)S(1)}, u32[]{:S(2)}, u32[]{:S(2)}) collective-permute-start(bf16[2,256,256]{1,2,0:T(8,128)(2,1)S(1)} %pad_maximum_fusion), channel_id=1, source_target_pairs={{0,7},{1,8},{2,9},{3,10},{4,11},{5,12},{6,13},{7,14},{8,15},{9,16}... | collective-permute-start | bytes 786440 | tf_op jit(solution)/shard_map/ppermute | solution.py:21
  120.0 3.4 collective-permute-start.8
  123.4 1.3 collective-permute-start.9
  124.8 5.5 %collective-permute-start.10 = (bf16[2,256,256]{1,2,0:T(8,128)(2,1)S(1)}, bf16[2,256,256]{1,2,0:T(8,128)(2,1)S(1)}, u32[]{:S(2)}, u32[]{:S(2)}) collective-permute-start(bf16[2,256,256]{1,2,0:T(8,128)(2,1)S(1)} %pad_maximum_fusion), channel_id=1, source_target_pairs={{0,10},{1,11},{2,12},{3,13},{4,14},{5,15},{6,16},{7,17},{8,18},{9,... | collective-permute-start | bytes 786440 | tf_op jit(solution)/shard_map/ppermute | solution.py:21
  130.3 16.4 %collective-permute-start.11 = (bf16[2,256,256]{1,2,0:T(8,128)(2,1)S(1)}, bf16[2,256,256]{1,2,0:T(8,128)(2,1)S(1)}, u32[]{:S(2)}, u32[]{:S(2)}) collective-permute-start(bf16[2,256,256]{1,2,0:T(8,128)(2,1)S(1)} %pad_maximum_fusion), channel_id=1, source_target_pairs={{0,11},{1,12},{2,13},{3,14},{4,15},{5,16},{6,17},{7,18},{8,19},{9,... | collective-permute-start | bytes 786440 | tf_op jit(solution)/shard_map/ppermute | solution.py:21
  146.7 2.8 collective-permute-start.12
  149.6 4.5 %collective-permute-start.13 = (bf16[2,256,256]{1,2,0:T(8,128)(2,1)S(1)}, bf16[2,256,256]{1,2,0:T(8,128)(2,1)S(1)}, u32[]{:S(2)}, u32[]{:S(2)}) collective-permute-start(bf16[2,256,256]{1,2,0:T(8,128)(2,1)S(1)} %pad_maximum_fusion), channel_id=1, source_target_pairs={{0,13},{1,14},{2,15},{3,16},{4,17},{5,18},{6,19},{7,20},{8,21},{9,... | collective-permute-start | bytes 786440 | tf_op jit(solution)/shard_map/ppermute | solution.py:21
  154.1 5.3 %collective-permute-start.14 = (bf16[2,256,256]{1,2,0:T(8,128)(2,1)S(1)}, bf16[2,256,256]{1,2,0:T(8,128)(2,1)S(1)}, u32[]{:S(2)}, u32[]{:S(2)}) collective-permute-start(bf16[2,256,256]{1,2,0:T(8,128)(2,1)S(1)} %pad_maximum_fusion), channel_id=1, source_target_pairs={{0,14},{1,15},{2,16},{3,17},{4,18},{5,19},{6,20},{7,21},{8,22},{9,... | collective-permute-start | bytes 786440 | tf_op jit(solution)/shard_map/ppermute | solution.py:21
  159.5 13.2 %collective-permute-start.15 = (bf16[2,256,256]{1,2,0:T(8,128)(2,1)S(1)}, bf16[2,256,256]{1,2,0:T(8,128)(2,1)S(1)}, u32[]{:S(2)}, u32[]{:S(2)}) collective-permute-start(bf16[2,256,256]{1,2,0:T(8,128)(2,1)S(1)} %pad_maximum_fusion), channel_id=1, source_target_pairs={{0,15},{1,16},{2,17},{3,18},{4,19},{5,20},{6,21},{7,22},{8,23},{9,... | collective-permute-start | bytes 786440 | tf_op jit(solution)/shard_map/ppermute | solution.py:21
  172.8 30.3 %collective-permute-start.16 = (bf16[2,256,256]{1,2,0:T(8,128)(2,1)S(1)}, bf16[2,256,256]{1,2,0:T(8,128)(2,1)S(1)}, u32[]{:S(2)}, u32[]{:S(2)}) collective-permute-start(bf16[2,256,256]{1,2,0:T(8,128)(2,1)S(1)} %pad_maximum_fusion), channel_id=1, source_target_pairs={{0,16},{1,17},{2,18},{3,19},{4,20},{5,21},{6,22},{7,23},{8,24},{9,... | collective-permute-start | bytes 786440 | tf_op jit(solution)/shard_map/ppermute | solution.py:21
  203.2 7.7 %collective-permute-done.15 = bf16[2,256,256]{1,2,0:T(8,128)(2,1)S(1)} collective-permute-done((bf16[2,256,256]{1,2,0:T(8,128)(2,1)S(1)}, bf16[2,256,256]{1,2,0:T(8,128)(2,1)S(1)}, u32[]{:S(2)}, u32[]{:S(2)}) %collective-permute-start.15) | collective-permute-done | bytes 262176 | tf_op jit(solution)/shard_map/ppermute | solution.py:21
  210.9 5.6 %collective-permute-done.16 = bf16[2,256,256]{1,2,0:T(8,128)(2,1)S(1)} collective-permute-done((bf16[2,256,256]{1,2,0:T(8,128)(2,1)S(1)}, bf16[2,256,256]{1,2,0:T(8,128)(2,1)S(1)}, u32[]{:S(2)}, u32[]{:S(2)}) %collective-permute-start.16) | collective-permute-done | bytes 262176 | tf_op jit(solution)/shard_map/ppermute | solution.py:21
  216.5 2.3 fusion.49
  218.9 4.1 %copy.25 = bf16[17,1,256,256]{3,2,0,1:T(8,128)(2,1)} copy(bf16[17,1,256,256]{2,3,1,0:T(8,128)(2,1)} %get-tuple-element.5) | data formatting | bytes 4456448 | tf_op jit(solution)/shard_map/slice | solution.py:102
  223.0 4.1 %copy.26 = bf16[17,1,256,256]{3,2,0,1:T(8,128)(2,1)} copy(bf16[17,1,256,256]{2,3,1,0:T(8,128)(2,1)} %get-tuple-element.6) | data formatting | bytes 4456448 | tf_op jit(solution)/shard_map/slice | solution.py:103
  227.1 3.3 fusion.52
  230.4 2.0 copy-done.3
  232.4 0.7 fusion.1
  233.2 6.4 %fusion.12 = f32[256,2560]{1,0:T(8,128)} fusion(bf16[256,2560]{1,0:T(8,128)(2,1)S(1)} %copy-done, bf16[4352,256]{1,0:T(8,128)(2,1)} %bitcast.54, f32[256,4352]{1,0:T(8,128)} %copy-done.3, f32[256]{0:T(256)S(1)} %fusion.1, f32[256]{0:T(256)S(1)} %get-tuple-element.17), kind=kOutput, calls=%fused_computation.23 | convolution fusion | flops 909377536 | bytes 10618880 | tf_op jit(solution)/shard_map/dot_general | solution.py:123
  239.6 0.0 all-reduce.2.cloned.1.call-update
  239.6 0.2 all-gather.5.cloned.1.call-start
  239.9 0.3 all-gather.5.cloned.1.call-update
  240.2 0.0 copy-done.11
  240.3 0.1 copy.28
  240.4 0.6 scatter_fusion
  241.0 0.0 copy-start.4
  241.1 145.7 %all-reduce.2.cloned.1.call-done = f32[256,2560]{1,0:T(8,128)} async-done(((f32[256,2560]{1,0:T(8,128)}), f32[256,2560]{1,0:T(8,128)}) %all-reduce.2.cloned.1.call-update) | async-done | bytes 2621456 | tf_op jit(solution)/shard_map/psum | solution.py:124
  386.7 2.1 multiply_reduce_fusion.1
  388.9 0.4 copy-done.1
  389.3 0.7 multiply_reduce_fusion
  390.0 0.0 all-gather.5.cloned.1.call-done
  390.0 4.1 %copy.29 = bf16[320,8,2,640]{3,1,2,0:T(8,128)(2,1)S(1)} copy(bf16[320,8,2,640]{3,2,1,0:T(2,128)(2,1)} %bitcast.52) | data formatting | bytes 13107200
  394.2 2.2 fusion.6
  396.4 1.0 fusion.21
  (67 shorter events, 0.6 us)
Async XLA Ops:
  8.0 225.2 %copy-start = (bf16[256,2560]{1,0:T(8,128)(2,1)S(1)}, bf16[256,2560]{1,0:T(8,128)(2,1)}, u32[]{:S(2)}) copy-start(bf16[256,2560]{1,0:T(8,128)(2,1)} %param.15) | copy-start | bytes 3932164
  8.0 54.5 %copy-start.9 = (f32[2560]{0:T(1024)S(1)}, f32[2560]{0:T(1024)}, u32[]{:S(2)}) copy-start(f32[2560]{0:T(1024)} %param.17) | copy-start | bytes 30724
  8.0 52.6 %all-gather.3.cloned.1.call-start = ((), (), s32[]{:S(2)}) async-start(), calls=%async_computation | async-start | bytes 1474560 | tf_op jit(solution)/shard_map/all_gather | solution.py:70
  8.8 378.0 %all-reduce.2.cloned.1.call-start = ((), (), s32[]{:S(2)}) async-start(), calls=%async_computation.1 | async-start | bytes 5242880 | tf_op jit(solution)/shard_map/psum | solution.py:124
  62.2 4.5 %copy-start.8 = (bf16[2560,256]{1,0:T(8,128)(2,1)S(1)}, bf16[2560,256]{1,0:T(8,128)(2,1)}, u32[]{:S(2)}) copy-start(bf16[2560,256]{1,0:T(8,128)(2,1)} %param.13) | copy-start | bytes 3932164
  64.7 2.8 copy-start.6
  64.7 7.0 %copy-start.7 = (f32[256]{0:T(256)S(1)}, f32[256]{0:T(256)}, u32[]{:S(2)}) copy-start(f32[256]{0:T(256)} %param.21) | copy-start | bytes 3076
  64.7 6.9 %collective-permute-start = (bf16[256,256]{0,1:T(8,128)(2,1)S(1)}, bf16[256,256]{0,1:T(8,128)(2,1)S(1)}, u32[]{:S(2)}, u32[]{:S(2)}) collective-permute-start(bf16[256,256]{0,1:T(8,128)(2,1)S(1)} %convolution_convert_fusion), channel_id=1, source_target_pairs={{0,64},{64,0},{128,192},{192,128},{1,65},{65,1},{129,193},{193,129... | collective-permute-start | bytes 393224 | tf_op jit(solution)/shard_map/ppermute | solution.py:15
  72.5 22.6 %collective-permute-start.1 = (bf16[2,256,256]{1,2,0:T(8,128)(2,1)S(1)}, bf16[2,256,256]{1,2,0:T(8,128)(2,1)S(1)}, u32[]{:S(2)}, u32[]{:S(2)}) collective-permute-start(bf16[2,256,256]{1,2,0:T(8,128)(2,1)S(1)} %pad_maximum_fusion), channel_id=1, source_target_pairs={{0,1},{1,2},{2,3},{3,4},{4,5},{5,6},{6,7},{7,8},{8,9},{9,10},{10,1... | collective-permute-start | bytes 786440 | tf_op jit(solution)/shard_map/ppermute | solution.py:21
  75.0 26.2 %collective-permute-start.2 = (bf16[2,256,256]{1,2,0:T(8,128)(2,1)S(1)}, bf16[2,256,256]{1,2,0:T(8,128)(2,1)S(1)}, u32[]{:S(2)}, u32[]{:S(2)}) collective-permute-start(bf16[2,256,256]{1,2,0:T(8,128)(2,1)S(1)} %pad_maximum_fusion), channel_id=1, source_target_pairs={{0,2},{1,3},{2,4},{3,5},{4,6},{5,7},{6,8},{7,9},{8,10},{9,11},{10,... | collective-permute-start | bytes 786440 | tf_op jit(solution)/shard_map/ppermute | solution.py:21
  79.6 40.3 %collective-permute-start.3 = (bf16[2,256,256]{1,2,0:T(8,128)(2,1)S(1)}, bf16[2,256,256]{1,2,0:T(8,128)(2,1)S(1)}, u32[]{:S(2)}, u32[]{:S(2)}) collective-permute-start(bf16[2,256,256]{1,2,0:T(8,128)(2,1)S(1)} %pad_maximum_fusion), channel_id=1, source_target_pairs={{0,3},{1,4},{2,5},{3,6},{4,7},{5,8},{6,9},{7,10},{8,11},{9,12},{10... | collective-permute-start | bytes 786440 | tf_op jit(solution)/shard_map/ppermute | solution.py:21
  84.9 38.5 %collective-permute-start.4 = (bf16[2,256,256]{1,2,0:T(8,128)(2,1)S(1)}, bf16[2,256,256]{1,2,0:T(8,128)(2,1)S(1)}, u32[]{:S(2)}, u32[]{:S(2)}) collective-permute-start(bf16[2,256,256]{1,2,0:T(8,128)(2,1)S(1)} %pad_maximum_fusion), channel_id=1, source_target_pairs={{0,4},{1,5},{2,6},{3,7},{4,8},{5,9},{6,10},{7,11},{8,12},{9,13},{1... | collective-permute-start | bytes 786440 | tf_op jit(solution)/shard_map/ppermute | solution.py:21
  90.3 34.4 %collective-permute-start.5 = (bf16[2,256,256]{1,2,0:T(8,128)(2,1)S(1)}, bf16[2,256,256]{1,2,0:T(8,128)(2,1)S(1)}, u32[]{:S(2)}, u32[]{:S(2)}) collective-permute-start(bf16[2,256,256]{1,2,0:T(8,128)(2,1)S(1)} %pad_maximum_fusion), channel_id=1, source_target_pairs={{0,5},{1,6},{2,7},{3,8},{4,9},{5,10},{6,11},{7,12},{8,13},{9,14},{... | collective-permute-start | bytes 786440 | tf_op jit(solution)/shard_map/ppermute | solution.py:21
  95.1 35.2 %collective-permute-start.6 = (bf16[2,256,256]{1,2,0:T(8,128)(2,1)S(1)}, bf16[2,256,256]{1,2,0:T(8,128)(2,1)S(1)}, u32[]{:S(2)}, u32[]{:S(2)}) collective-permute-start(bf16[2,256,256]{1,2,0:T(8,128)(2,1)S(1)} %pad_maximum_fusion), channel_id=1, source_target_pairs={{0,6},{1,7},{2,8},{3,9},{4,10},{5,11},{6,12},{7,13},{8,14},{9,15},... | collective-permute-start | bytes 786440 | tf_op jit(solution)/shard_map/ppermute | solution.py:21
  101.2 45.6 %collective-permute-start.7 = (bf16[2,256,256]{1,2,0:T(8,128)(2,1)S(1)}, bf16[2,256,256]{1,2,0:T(8,128)(2,1)S(1)}, u32[]{:S(2)}, u32[]{:S(2)}) collective-permute-start(bf16[2,256,256]{1,2,0:T(8,128)(2,1)S(1)} %pad_maximum_fusion), channel_id=1, source_target_pairs={{0,7},{1,8},{2,9},{3,10},{4,11},{5,12},{6,13},{7,14},{8,15},{9,16}... | collective-permute-start | bytes 786440 | tf_op jit(solution)/shard_map/ppermute | solution.py:21
  120.0 29.6 %collective-permute-start.8 = (bf16[2,256,256]{1,2,0:T(8,128)(2,1)S(1)}, bf16[2,256,256]{1,2,0:T(8,128)(2,1)S(1)}, u32[]{:S(2)}, u32[]{:S(2)}) collective-permute-start(bf16[2,256,256]{1,2,0:T(8,128)(2,1)S(1)} %pad_maximum_fusion), channel_id=1, source_target_pairs={{0,8},{1,9},{2,10},{3,11},{4,12},{5,13},{6,14},{7,15},{8,16},{9,17... | collective-permute-start | bytes 786440 | tf_op jit(solution)/shard_map/ppermute | solution.py:21
  123.4 30.7 %collective-permute-start.9 = (bf16[2,256,256]{1,2,0:T(8,128)(2,1)S(1)}, bf16[2,256,256]{1,2,0:T(8,128)(2,1)S(1)}, u32[]{:S(2)}, u32[]{:S(2)}) collective-permute-start(bf16[2,256,256]{1,2,0:T(8,128)(2,1)S(1)} %pad_maximum_fusion), channel_id=1, source_target_pairs={{0,9},{1,10},{2,11},{3,12},{4,13},{5,14},{6,15},{7,16},{8,17},{9,1... | collective-permute-start | bytes 786440 | tf_op jit(solution)/shard_map/ppermute | solution.py:21
  124.8 34.7 %collective-permute-start.10 = (bf16[2,256,256]{1,2,0:T(8,128)(2,1)S(1)}, bf16[2,256,256]{1,2,0:T(8,128)(2,1)S(1)}, u32[]{:S(2)}, u32[]{:S(2)}) collective-permute-start(bf16[2,256,256]{1,2,0:T(8,128)(2,1)S(1)} %pad_maximum_fusion), channel_id=1, source_target_pairs={{0,10},{1,11},{2,12},{3,13},{4,14},{5,15},{6,16},{7,17},{8,18},{9,... | collective-permute-start | bytes 786440 | tf_op jit(solution)/shard_map/ppermute | solution.py:21
  130.3 42.5 %collective-permute-start.11 = (bf16[2,256,256]{1,2,0:T(8,128)(2,1)S(1)}, bf16[2,256,256]{1,2,0:T(8,128)(2,1)S(1)}, u32[]{:S(2)}, u32[]{:S(2)}) collective-permute-start(bf16[2,256,256]{1,2,0:T(8,128)(2,1)S(1)} %pad_maximum_fusion), channel_id=1, source_target_pairs={{0,11},{1,12},{2,13},{3,14},{4,15},{5,16},{6,17},{7,18},{8,19},{9,... | collective-permute-start | bytes 786440 | tf_op jit(solution)/shard_map/ppermute | solution.py:21
  146.7 56.4 %collective-permute-start.12 = (bf16[2,256,256]{1,2,0:T(8,128)(2,1)S(1)}, bf16[2,256,256]{1,2,0:T(8,128)(2,1)S(1)}, u32[]{:S(2)}, u32[]{:S(2)}) collective-permute-start(bf16[2,256,256]{1,2,0:T(8,128)(2,1)S(1)} %pad_maximum_fusion), channel_id=1, source_target_pairs={{0,12},{1,13},{2,14},{3,15},{4,16},{5,17},{6,18},{7,19},{8,20},{9,... | collective-permute-start | bytes 786440 | tf_op jit(solution)/shard_map/ppermute | solution.py:21
  149.6 53.6 %collective-permute-start.13 = (bf16[2,256,256]{1,2,0:T(8,128)(2,1)S(1)}, bf16[2,256,256]{1,2,0:T(8,128)(2,1)S(1)}, u32[]{:S(2)}, u32[]{:S(2)}) collective-permute-start(bf16[2,256,256]{1,2,0:T(8,128)(2,1)S(1)} %pad_maximum_fusion), channel_id=1, source_target_pairs={{0,13},{1,14},{2,15},{3,16},{4,17},{5,18},{6,19},{7,20},{8,21},{9,... | collective-permute-start | bytes 786440 | tf_op jit(solution)/shard_map/ppermute | solution.py:21
  154.1 49.1 %collective-permute-start.14 = (bf16[2,256,256]{1,2,0:T(8,128)(2,1)S(1)}, bf16[2,256,256]{1,2,0:T(8,128)(2,1)S(1)}, u32[]{:S(2)}, u32[]{:S(2)}) collective-permute-start(bf16[2,256,256]{1,2,0:T(8,128)(2,1)S(1)} %pad_maximum_fusion), channel_id=1, source_target_pairs={{0,14},{1,15},{2,16},{3,17},{4,18},{5,19},{6,20},{7,21},{8,22},{9,... | collective-permute-start | bytes 786440 | tf_op jit(solution)/shard_map/ppermute | solution.py:21
  159.5 51.4 %collective-permute-start.15 = (bf16[2,256,256]{1,2,0:T(8,128)(2,1)S(1)}, bf16[2,256,256]{1,2,0:T(8,128)(2,1)S(1)}, u32[]{:S(2)}, u32[]{:S(2)}) collective-permute-start(bf16[2,256,256]{1,2,0:T(8,128)(2,1)S(1)} %pad_maximum_fusion), channel_id=1, source_target_pairs={{0,15},{1,16},{2,17},{3,18},{4,19},{5,20},{6,21},{7,22},{8,23},{9,... | collective-permute-start | bytes 786440 | tf_op jit(solution)/shard_map/ppermute | solution.py:21
  172.8 43.8 %collective-permute-start.16 = (bf16[2,256,256]{1,2,0:T(8,128)(2,1)S(1)}, bf16[2,256,256]{1,2,0:T(8,128)(2,1)S(1)}, u32[]{:S(2)}, u32[]{:S(2)}) collective-permute-start(bf16[2,256,256]{1,2,0:T(8,128)(2,1)S(1)} %pad_maximum_fusion), channel_id=1, source_target_pairs={{0,16},{1,17},{2,18},{3,19},{4,20},{5,21},{6,22},{7,23},{8,24},{9,... | collective-permute-start | bytes 786440 | tf_op jit(solution)/shard_map/ppermute | solution.py:21
  230.4 2.0 copy-start.3
  239.6 0.7 copy-start.11
  239.6 149.3 %copy-start.5 = (f32[2560]{0:T(1024)S(1)}, f32[2560]{0:T(1024)}, u32[]{:S(2)}) copy-start(f32[2560]{0:T(1024)} %param.18) | copy-start | bytes 30724
  239.6 150.4 %all-gather.5.cloned.1.call-start = ((), (), s32[]{:S(2)}) async-start(), calls=%async_computation.2 | async-start | bytes 6656000 | tf_op jit(solution)/shard_map/all_gather | solution.py:127
  241.0 148.9 %copy-start.4 = (bf16[2,128,256]{2,1,0:T(8,128)(2,1)}, bf16[2,128,256]{2,1,0:T(8,128)(2,1)S(1)}, u32[]{:S(2)}) copy-start(bf16[2,128,256]{2,1,0:T(8,128)(2,1)S(1)} %scatter_fusion) | copy-start | bytes 393220
  386.7 2.5 copy-start.1
  390.0 4.2 %copy-start.2 = (f32[256,2560]{1,0:T(8,128)S(1)}, f32[256,2560]{1,0:T(8,128)}, u32[]{:S(2)}) copy-start(f32[256,2560]{1,0:T(8,128)} %all-reduce.2.cloned.1.call-done) | copy-start | bytes 7864324
  390.0 4.2 %copy-start.10 = (f32[2560]{0:T(1024)S(1)}, f32[2560]{0:T(1024)}, u32[]{:S(2)}) copy-start(f32[2560]{0:T(1024)} %param.19) | copy-start | bytes 30724
Sparse Core Ops, SparseCore 0:
  10.9 49.6 all-gather.2
  239.8 146.9 all-reduce.1
Sparse Core Ops, SparseCore 1:
  243.4 133.3 all-gather.4
where the time goes:
time: 406 us; the launch traced here: 405 us
  waiting for transfers between devices  214 us (53%)
  starting transfers between devices  132 us (33%)
  local copies, waits for them, and re-layouts  19.8 us (5%)
  between operations  16.2 us (4%)
  matrix products  14.9 us (4%)
  other arithmetic  8.28 us (2%)
    psum x1, waiting for transfers between devices, local(): attended = lax.psum(head_terms, ('section', 'tensor'))  146 us
    ppermute x16, starting transfers between devices, shifted(): return lax.ppermute(block, axis, route)  130 us
    all_gather x1, waiting for transfers between devices, local(): features = lax.all_gather(tokens, ('section', 'tensor'), axis=1, tiled=True)  49.9 us
    ppermute x16, waiting for transfers between devices, shifted(): return lax.ppermute(block, axis, route)  13.3 us
  transfers between devices with their start and end apart: 20, of which 5 were waited for; matrix products, arithmetic and copies ran while one was open for 2% of the time, Pallas kernels for 0%

commit v1 on v0

--- a/solution.py
+++ b/solution.py
@@ -67,7 +67,15 @@
     halfway = head_width // 2
     unit_count = w_gateup.shape[2]
     span_blocks = min(REACH, lax.axis_size("seq") // 2)
-    features = lax.all_gather(tokens, ("section", "tensor"), axis=1, tiled=True)
+    features = jnp.concatenate(
+        lax.all_to_all(
+            jnp.stack(tuple((tokens for _ in range(lax.axis_size(("section", "tensor"))))), axis=0),
+            ("section", "tensor"),
+            0,
+            0,
+        ),
+        axis=1,
+    )
     first_row = lax.axis_index("seq") * row_count
     prompt_ends = jnp.cumsum(prompt_lengths)
     prompt_starts = prompt_ends - prompt_lengths

time: 406 us -> 383 us (0.943)
  waiting for transfers between devices: 214 us -> 199 us
  starting transfers between devices: 132 us -> 119 us
  other arithmetic: 8.28 us -> 12.5 us
    all_gather x1 -> x0, waiting for transfers between devices: 49.9 us -> none  [local(): features = lax.all_gather(tokens, ('section', 'tensor'), axis=1, tiled=True)]
    ppermute x16, waiting for transfers between devices: 13.3 us -> 41.3 us  [shifted(): return lax.ppermute(block, axis, route)]
    ppermute x16, starting transfers between devices: 130 us -> 110 us  [shifted(): return lax.ppermute(block, axis, route)]
    all_to_all x0 -> x1, waiting for transfers between devices: none -> 16.3 us  [local(): lax.all_to_all(jnp.stack(tuple((tokens for _ in range(lax.axis_size(('sec...]
    psum x1, waiting for transfers between devices: 146 us -> 138 us  [local(): attended = lax.psum(head_terms, ('section', 'tensor'))]
    all_to_all x0 -> x1, starting transfers between devices: none -> 6.11 us  [local(): lax.all_to_all(jnp.stack(tuple((tokens for _ in range(lax.axis_size(('sec...]
  transfers between devices with their start and end apart: 20 -> 20, of which waited for: 5 -> 7; matrix products, arithmetic and copies ran while one was open for 2% -> 3% of each run, Pallas kernels for 0% -> 0%
where the time goes in v1:
time: 383 us; the launch traced here: 382 us
  waiting for transfers between devices  199 us (52%)
  starting transfers between devices  119 us (31%)
  local copies, waits for them, and re-layouts  22.2 us (6%)
  between operations  16.2 us (4%)
  matrix products  12.6 us (3%)
  other arithmetic  12.5 us (3%)
    psum x1, waiting for transfers between devices, local(): attended = lax.psum(head_terms, ('section', 'tensor'))  138 us
    ppermute x16, starting transfers between devices, shifted(): return lax.ppermute(block, axis, route)  110 us
    ppermute x16, waiting for transfers between devices, shifted(): return lax.ppermute(block, axis, route)  41.3 us
    all_to_all x1, waiting for transfers between devices, local(): lax.all_to_all(jnp.stack(tuple((tokens for _ in range(lax.axis_size(('sec...  16.3 us
    unnamed x56, local copies, waits for them, and re-layouts  7.89 us
  transfers between devices with their start and end apart: 20, of which 7 were waited for; matrix products, arithmetic and copies ran while one was open for 3% of the time, Pallas kernels for 0%

profile of v1, /device:TPU:8, one launch (start us, length us, event | category | flops | bytes accessed | tf_op | source)
XLA Modules:
  0.0 381.6 jit_solution(7420378365079664568)
XLA Ops:
  8.0 2.2 stack.72
  10.2 6.1 %all-to-all-start = ((bf16[8,256,320]{1,2,0:T(8,128)(2,1)}), bf16[8,256,320]{1,2,0:T(8,128)(2,1)S(1)}, u32[]{:S(2)}, u32[]{:S(2)}) async-start(bf16[8,256,320]{1,2,0:T(8,128)(2,1)} %stack.72), calls=%async_computation | async-start | bytes 2621440 | tf_op jit(solution)/shard_map/all_to_all | solution.py:71
  16.3 0.0 all-reduce.2.cloned.1.call-start
  16.4 0.2 reduce-window.8
  16.6 0.1 iota_add_fusion
  16.7 0.1 convert_reduce_fusion.1
  16.8 0.1 select_reduce_fusion
  16.8 0.1 convert_reduce_fusion
  17.0 0.6 compare_select_fusion
  17.6 16.3 %all-to-all-done = bf16[8,256,320]{1,2,0:T(8,128)(2,1)S(1)} async-done(((bf16[8,256,320]{1,2,0:T(8,128)(2,1)}), bf16[8,256,320]{1,2,0:T(8,128)(2,1)S(1)}, u32[]{:S(2)}, u32[]{:S(2)}) %all-to-all-start) | async-done | bytes 1310752 | tf_op jit(solution)/shard_map/all_to_all | solution.py:71
  33.9 0.4 multiply_reduce_fusion.2
  34.3 1.9 multiply_convert_fusion.1
  36.2 0.6 convolution_convert_fusion
  36.9 2.9 collective-permute-start
  39.8 0.7 multiply_reduce_fusion.3
  40.5 0.1 multiply_multiply_fusion.1
  40.6 3.4 collective-permute-done
  44.1 0.1 fusion.17
  44.2 0.1 fusion.18
  44.3 1.2 broadcast_select_fusion.2
  45.6 1.9 collective-permute-start.1
  47.5 1.2 fusion.28
  48.7 6.1 %collective-permute-start.2 = (bf16[2,256,256]{1,2,0:T(8,128)(2,1)S(1)}, bf16[2,256,256]{1,2,0:T(8,128)(2,1)S(1)}, u32[]{:S(2)}, u32[]{:S(2)}) collective-permute-start(bf16[2,256,256]{1,2,0:T(8,128)(2,1)S(1)} %pad_maximum_fusion), channel_id=1, source_target_pairs={{0,2},{1,3},{2,4},{3,5},{4,6},{5,7},{6,8},{7,9},{8,10},{9,11},{10,... | collective-permute-start | bytes 786440 | tf_op jit(solution)/shard_map/ppermute | solution.py:21
  54.8 8.2 %collective-permute-start.3 = (bf16[2,256,256]{1,2,0:T(8,128)(2,1)S(1)}, bf16[2,256,256]{1,2,0:T(8,128)(2,1)S(1)}, u32[]{:S(2)}, u32[]{:S(2)}) collective-permute-start(bf16[2,256,256]{1,2,0:T(8,128)(2,1)S(1)} %pad_maximum_fusion), channel_id=1, source_target_pairs={{0,3},{1,4},{2,5},{3,6},{4,7},{5,8},{6,9},{7,10},{8,11},{9,12},{10... | collective-permute-start | bytes 786440 | tf_op jit(solution)/shard_map/ppermute | solution.py:21
  63.0 2.5 collective-permute-start.4
  65.6 7.7 %collective-permute-start.5 = (bf16[2,256,256]{1,2,0:T(8,128)(2,1)S(1)}, bf16[2,256,256]{1,2,0:T(8,128)(2,1)S(1)}, u32[]{:S(2)}, u32[]{:S(2)}) collective-permute-start(bf16[2,256,256]{1,2,0:T(8,128)(2,1)S(1)} %pad_maximum_fusion), channel_id=1, source_target_pairs={{0,5},{1,6},{2,7},{3,8},{4,9},{5,10},{6,11},{7,12},{8,13},{9,14},{... | collective-permute-start | bytes 786440 | tf_op jit(solution)/shard_map/ppermute | solution.py:21
  73.3 4.7 %collective-permute-start.6 = (bf16[2,256,256]{1,2,0:T(8,128)(2,1)S(1)}, bf16[2,256,256]{1,2,0:T(8,128)(2,1)S(1)}, u32[]{:S(2)}, u32[]{:S(2)}) collective-permute-start(bf16[2,256,256]{1,2,0:T(8,128)(2,1)S(1)} %pad_maximum_fusion), channel_id=1, source_target_pairs={{0,6},{1,7},{2,8},{3,9},{4,10},{5,11},{6,12},{7,13},{8,14},{9,15},... | collective-permute-start | bytes 786440 | tf_op jit(solution)/shard_map/ppermute | solution.py:21
  78.0 19.3 %collective-permute-start.7 = (bf16[2,256,256]{1,2,0:T(8,128)(2,1)S(1)}, bf16[2,256,256]{1,2,0:T(8,128)(2,1)S(1)}, u32[]{:S(2)}, u32[]{:S(2)}) collective-permute-start(bf16[2,256,256]{1,2,0:T(8,128)(2,1)S(1)} %pad_maximum_fusion), channel_id=1, source_target_pairs={{0,7},{1,8},{2,9},{3,10},{4,11},{5,12},{6,13},{7,14},{8,15},{9,16}... | collective-permute-start | bytes 786440 | tf_op jit(solution)/shard_map/ppermute | solution.py:21
  97.3 3.5 collective-permute-start.8
  100.8 1.3 collective-permute-start.9
  102.2 3.7 collective-permute-start.10
  105.9 19.1 %collective-permute-start.11 = (bf16[2,256,256]{1,2,0:T(8,128)(2,1)S(1)}, bf16[2,256,256]{1,2,0:T(8,128)(2,1)S(1)}, u32[]{:S(2)}, u32[]{:S(2)}) collective-permute-start(bf16[2,256,256]{1,2,0:T(8,128)(2,1)S(1)} %pad_maximum_fusion), channel_id=1, source_target_pairs={{0,11},{1,12},{2,13},{3,14},{4,15},{5,16},{6,17},{7,18},{8,19},{9,... | collective-permute-start | bytes 786440 | tf_op jit(solution)/shard_map/ppermute | solution.py:21
  125.0 3.2 collective-permute-start.12
  128.2 4.2 %collective-permute-start.13 = (bf16[2,256,256]{1,2,0:T(8,128)(2,1)S(1)}, bf16[2,256,256]{1,2,0:T(8,128)(2,1)S(1)}, u32[]{:S(2)}, u32[]{:S(2)}) collective-permute-start(bf16[2,256,256]{1,2,0:T(8,128)(2,1)S(1)} %pad_maximum_fusion), channel_id=1, source_target_pairs={{0,13},{1,14},{2,15},{3,16},{4,17},{5,18},{6,19},{7,20},{8,21},{9,... | collective-permute-start | bytes 786440 | tf_op jit(solution)/shard_map/ppermute | solution.py:21
  132.5 2.3 collective-permute-start.14
  134.9 10.5 %collective-permute-start.15 = (bf16[2,256,256]{1,2,0:T(8,128)(2,1)S(1)}, bf16[2,256,256]{1,2,0:T(8,128)(2,1)S(1)}, u32[]{:S(2)}, u32[]{:S(2)}) collective-permute-start(bf16[2,256,256]{1,2,0:T(8,128)(2,1)S(1)} %pad_maximum_fusion), channel_id=1, source_target_pairs={{0,15},{1,16},{2,17},{3,18},{4,19},{5,20},{6,21},{7,22},{8,23},{9,... | collective-permute-start | bytes 786440 | tf_op jit(solution)/shard_map/ppermute | solution.py:21
  145.4 11.5 %collective-permute-start.16 = (bf16[2,256,256]{1,2,0:T(8,128)(2,1)S(1)}, bf16[2,256,256]{1,2,0:T(8,128)(2,1)S(1)}, u32[]{:S(2)}, u32[]{:S(2)}) collective-permute-start(bf16[2,256,256]{1,2,0:T(8,128)(2,1)S(1)} %pad_maximum_fusion), channel_id=1, source_target_pairs={{0,16},{1,17},{2,18},{3,19},{4,20},{5,21},{6,22},{7,23},{8,24},{9,... | collective-permute-start | bytes 786440 | tf_op jit(solution)/shard_map/ppermute | solution.py:21
  157.0 4.3 %collective-permute-done.13 = bf16[2,256,256]{1,2,0:T(8,128)(2,1)S(1)} collective-permute-done((bf16[2,256,256]{1,2,0:T(8,128)(2,1)S(1)}, bf16[2,256,256]{1,2,0:T(8,128)(2,1)S(1)}, u32[]{:S(2)}, u32[]{:S(2)}) %collective-permute-start.13) | collective-permute-done | bytes 262176 | tf_op jit(solution)/shard_map/ppermute | solution.py:21
  161.3 17.0 %collective-permute-done.14 = bf16[2,256,256]{1,2,0:T(8,128)(2,1)S(1)} collective-permute-done((bf16[2,256,256]{1,2,0:T(8,128)(2,1)S(1)}, bf16[2,256,256]{1,2,0:T(8,128)(2,1)S(1)}, u32[]{:S(2)}, u32[]{:S(2)}) %collective-permute-start.14) | collective-permute-done | bytes 262176 | tf_op jit(solution)/shard_map/ppermute | solution.py:21
  178.3 14.4 %collective-permute-done.15 = bf16[2,256,256]{1,2,0:T(8,128)(2,1)S(1)} collective-permute-done((bf16[2,256,256]{1,2,0:T(8,128)(2,1)S(1)}, bf16[2,256,256]{1,2,0:T(8,128)(2,1)S(1)}, u32[]{:S(2)}, u32[]{:S(2)}) %collective-permute-start.15) | collective-permute-done | bytes 262176 | tf_op jit(solution)/shard_map/ppermute | solution.py:21
  192.8 5.6 %collective-permute-done.16 = bf16[2,256,256]{1,2,0:T(8,128)(2,1)S(1)} collective-permute-done((bf16[2,256,256]{1,2,0:T(8,128)(2,1)S(1)}, bf16[2,256,256]{1,2,0:T(8,128)(2,1)S(1)}, u32[]{:S(2)}, u32[]{:S(2)}) %collective-permute-start.16) | collective-permute-done | bytes 262176 | tf_op jit(solution)/shard_map/ppermute | solution.py:21
  198.4 1.6 fusion.41
  200.0 4.1 %copy.24 = bf16[17,1,256,256]{3,2,0,1:T(8,128)(2,1)} copy(bf16[17,1,256,256]{2,3,1,0:T(8,128)(2,1)} %get-tuple-element.7) | data formatting | bytes 4456448 | tf_op jit(solution)/shard_map/slice | solution.py:110
  204.1 2.4 copy.25
  206.6 3.4 fusion.44
  210.0 2.3 copy-done.4
  212.2 0.7 fusion.1
  213.0 0.2 copy-done.5
  213.2 5.7 %fusion.7 = f32[256,2560]{1,0:T(8,128)} fusion(bf16[256,2560]{1,0:T(8,128)(2,1)S(1)} %copy-done, bf16[4352,256]{1,0:T(8,128)(2,1)S(1)} %bitcast.61, f32[256,4352]{1,0:T(8,128)} %copy-done.4, f32[256]{0:T(256)S(1)} %fusion.1, f32[256]{0:T(256)S(1)} %get-tuple-element.19), kind=kOutput, calls=%fused_computation.18 | convolution fusion | flops 909377536 | bytes 10618880 | tf_op jit(solution)/shard_map/dot_general | solution.py:131
  219.0 0.2 all-gather.2.cloned.1.call-start
  219.2 0.3 all-gather.2.cloned.1.call-update
  219.5 0.0 copy-done.19
  219.6 0.3 copy-done.8
  219.9 3.2 copy.26
  223.1 0.1 copy.28
  223.2 0.6 scatter_fusion
  223.9 137.8 %all-reduce.2.cloned.1.call-done = f32[256,2560]{1,0:T(8,128)} async-done(((f32[256,2560]{1,0:T(8,128)}), f32[256,2560]{1,0:T(8,128)}) %all-reduce.2.cloned.1.call-update) | async-done | bytes 2621456 | tf_op jit(solution)/shard_map/psum | solution.py:132
  361.7 2.1 multiply_reduce_fusion.1
  363.8 0.4 copy-done.1
  364.2 2.4 multiply_reduce_fusion
  366.7 4.1 %copy.29 = bf16[320,8,2,640]{3,1,2,0:T(8,128)(2,1)S(1)} copy(bf16[320,8,2,640]{3,2,1,0:T(2,128)(2,1)} %bitcast.60) | data formatting | bytes 13107200
  370.8 0.2 copy-done.3
  371.1 2.1 fusion.3
  373.2 1.0 fusion.16
  (84 shorter events, 0.7 us)
Async XLA Ops:
  8.0 205.0 %copy-start = (bf16[256,2560]{1,0:T(8,128)(2,1)S(1)}, bf16[256,2560]{1,0:T(8,128)(2,1)}, u32[]{:S(2)}) copy-start(bf16[256,2560]{1,0:T(8,128)(2,1)} %param.15) | copy-start | bytes 3932164
  8.0 8.4 %copy-start.18 = (s32[8]{0:T(128)S(1)}, s32[8]{0:T(128)}, u32[]{:S(2)}) copy-start(s32[8]{0:T(128)} %param.22) | copy-start | bytes 100
  8.0 26.3 %copy-start.12 = (f32[2560]{0:T(1024)S(1)}, f32[2560]{0:T(1024)}, u32[]{:S(2)}) copy-start(f32[2560]{0:T(1024)} %param.17) | copy-start | bytes 30724
  10.2 23.7 %all-to-all-start = ((bf16[8,256,320]{1,2,0:T(8,128)(2,1)}), bf16[8,256,320]{1,2,0:T(8,128)(2,1)S(1)}, u32[]{:S(2)}, u32[]{:S(2)}) async-start(bf16[8,256,320]{1,2,0:T(8,128)(2,1)} %stack.72), calls=%async_computation | async-start | bytes 2621440 | tf_op jit(solution)/shard_map/all_to_all | solution.py:71
  16.3 345.4 %all-reduce.2.cloned.1.call-start = ((), (), s32[]{:S(2)}) async-start(), calls=%async_computation.1 | async-start | bytes 5242880 | tf_op jit(solution)/shard_map/psum | solution.py:132
  16.6 19.6 %copy-start.10 = (s32[4352]{0:T(1024)}, s32[4352]{0:T(1024)S(1)}, u32[]{:S(2)}) copy-start(s32[4352]{0:T(1024)S(1)} %add.111) | copy-start | bytes 52228
  34.3 1.9 copy-start.16
  36.2 3.6 copy-start.17
  36.2 4.3 %copy-start.14 = (f32[256]{0:T(256)S(1)}, f32[256]{0:T(256)}, u32[]{:S(2)}) copy-start(f32[256]{0:T(256)} %param.20) | copy-start | bytes 3076
  36.9 7.4 %copy-start.7 = (bf16[256,256]{0,1:T(8,128)(2,1)}, bf16[256,256]{0,1:T(8,128)(2,1)S(1)}, u32[]{:S(2)}) copy-start(bf16[256,256]{0,1:T(8,128)(2,1)S(1)} %convolution_convert_fusion) | copy-start | bytes 393220
  36.9 7.3 %copy-start.15 = (f32[256]{0:T(256)S(1)}, f32[256]{0:T(256)}, u32[]{:S(2)}) copy-start(f32[256]{0:T(256)} %param.21) | copy-start | bytes 3076
  36.9 7.1 %collective-permute-start = (bf16[256,256]{0,1:T(8,128)(2,1)S(1)}, bf16[256,256]{0,1:T(8,128)(2,1)S(1)}, u32[]{:S(2)}, u32[]{:S(2)}) collective-permute-start(bf16[256,256]{0,1:T(8,128)(2,1)S(1)} %convolution_convert_fusion), channel_id=1, source_target_pairs={{0,64},{64,0},{128,192},{192,128},{1,65},{65,1},{129,193},{193,129... | collective-permute-start | bytes 393224 | tf_op jit(solution)/shard_map/ppermute | solution.py:15
  45.6 27.7 %collective-permute-start.1 = (bf16[2,256,256]{1,2,0:T(8,128)(2,1)S(1)}, bf16[2,256,256]{1,2,0:T(8,128)(2,1)S(1)}, u32[]{:S(2)}, u32[]{:S(2)}) collective-permute-start(bf16[2,256,256]{1,2,0:T(8,128)(2,1)S(1)} %pad_maximum_fusion), channel_id=1, source_target_pairs={{0,1},{1,2},{2,3},{3,4},{4,5},{5,6},{6,7},{7,8},{8,9},{9,10},{10,1... | collective-permute-start | bytes 786440 | tf_op jit(solution)/shard_map/ppermute | solution.py:21
  48.7 29.3 %collective-permute-start.2 = (bf16[2,256,256]{1,2,0:T(8,128)(2,1)S(1)}, bf16[2,256,256]{1,2,0:T(8,128)(2,1)S(1)}, u32[]{:S(2)}, u32[]{:S(2)}) collective-permute-start(bf16[2,256,256]{1,2,0:T(8,128)(2,1)S(1)} %pad_maximum_fusion), channel_id=1, source_target_pairs={{0,2},{1,3},{2,4},{3,5},{4,6},{5,7},{6,8},{7,9},{8,10},{9,11},{10,... | collective-permute-start | bytes 786440 | tf_op jit(solution)/shard_map/ppermute | solution.py:21
  54.8 42.5 %collective-permute-start.3 = (bf16[2,256,256]{1,2,0:T(8,128)(2,1)S(1)}, bf16[2,256,256]{1,2,0:T(8,128)(2,1)S(1)}, u32[]{:S(2)}, u32[]{:S(2)}) collective-permute-start(bf16[2,256,256]{1,2,0:T(8,128)(2,1)S(1)} %pad_maximum_fusion), channel_id=1, source_target_pairs={{0,3},{1,4},{2,5},{3,6},{4,7},{5,8},{6,9},{7,10},{8,11},{9,12},{10... | collective-permute-start | bytes 786440 | tf_op jit(solution)/shard_map/ppermute | solution.py:21
  63.0 37.8 %collective-permute-start.4 = (bf16[2,256,256]{1,2,0:T(8,128)(2,1)S(1)}, bf16[2,256,256]{1,2,0:T(8,128)(2,1)S(1)}, u32[]{:S(2)}, u32[]{:S(2)}) collective-permute-start(bf16[2,256,256]{1,2,0:T(8,128)(2,1)S(1)} %pad_maximum_fusion), channel_id=1, source_target_pairs={{0,4},{1,5},{2,6},{3,7},{4,8},{5,9},{6,10},{7,11},{8,12},{9,13},{1... | collective-permute-start | bytes 786440 | tf_op jit(solution)/shard_map/ppermute | solution.py:21
  65.6 36.6 %collective-permute-start.5 = (bf16[2,256,256]{1,2,0:T(8,128)(2,1)S(1)}, bf16[2,256,256]{1,2,0:T(8,128)(2,1)S(1)}, u32[]{:S(2)}, u32[]{:S(2)}) collective-permute-start(bf16[2,256,256]{1,2,0:T(8,128)(2,1)S(1)} %pad_maximum_fusion), channel_id=1, source_target_pairs={{0,5},{1,6},{2,7},{3,8},{4,9},{5,10},{6,11},{7,12},{8,13},{9,14},{... | collective-permute-start | bytes 786440 | tf_op jit(solution)/shard_map/ppermute | solution.py:21
  73.3 32.6 %collective-permute-start.6 = (bf16[2,256,256]{1,2,0:T(8,128)(2,1)S(1)}, bf16[2,256,256]{1,2,0:T(8,128)(2,1)S(1)}, u32[]{:S(2)}, u32[]{:S(2)}) collective-permute-start(bf16[2,256,256]{1,2,0:T(8,128)(2,1)S(1)} %pad_maximum_fusion), channel_id=1, source_target_pairs={{0,6},{1,7},{2,8},{3,9},{4,10},{5,11},{6,12},{7,13},{8,14},{9,15},... | collective-permute-start | bytes 786440 | tf_op jit(solution)/shard_map/ppermute | solution.py:21
  78.0 47.0 %collective-permute-start.7 = (bf16[2,256,256]{1,2,0:T(8,128)(2,1)S(1)}, bf16[2,256,256]{1,2,0:T(8,128)(2,1)S(1)}, u32[]{:S(2)}, u32[]{:S(2)}) collective-permute-start(bf16[2,256,256]{1,2,0:T(8,128)(2,1)S(1)} %pad_maximum_fusion), channel_id=1, source_target_pairs={{0,7},{1,8},{2,9},{3,10},{4,11},{5,12},{6,13},{7,14},{8,15},{9,16}... | collective-permute-start | bytes 786440 | tf_op jit(solution)/shard_map/ppermute | solution.py:21
  97.3 30.9 %collective-permute-start.8 = (bf16[2,256,256]{1,2,0:T(8,128)(2,1)S(1)}, bf16[2,256,256]{1,2,0:T(8,128)(2,1)S(1)}, u32[]{:S(2)}, u32[]{:S(2)}) collective-permute-start(bf16[2,256,256]{1,2,0:T(8,128)(2,1)S(1)} %pad_maximum_fusion), channel_id=1, source_target_pairs={{0,8},{1,9},{2,10},{3,11},{4,12},{5,13},{6,14},{7,15},{8,16},{9,17... | collective-permute-start | bytes 786440 | tf_op jit(solution)/shard_map/ppermute | solution.py:21
  100.8 31.7 %collective-permute-start.9 = (bf16[2,256,256]{1,2,0:T(8,128)(2,1)S(1)}, bf16[2,256,256]{1,2,0:T(8,128)(2,1)S(1)}, u32[]{:S(2)}, u32[]{:S(2)}) collective-permute-start(bf16[2,256,256]{1,2,0:T(8,128)(2,1)S(1)} %pad_maximum_fusion), channel_id=1, source_target_pairs={{0,9},{1,10},{2,11},{3,12},{4,13},{5,14},{6,15},{7,16},{8,17},{9,1... | collective-permute-start | bytes 786440 | tf_op jit(solution)/shard_map/ppermute | solution.py:21
  102.2 32.7 %collective-permute-start.10 = (bf16[2,256,256]{1,2,0:T(8,128)(2,1)S(1)}, bf16[2,256,256]{1,2,0:T(8,128)(2,1)S(1)}, u32[]{:S(2)}, u32[]{:S(2)}) collective-permute-start(bf16[2,256,256]{1,2,0:T(8,128)(2,1)S(1)} %pad_maximum_fusion), channel_id=1, source_target_pairs={{0,10},{1,11},{2,12},{3,13},{4,14},{5,15},{6,16},{7,17},{8,18},{9,... | collective-permute-start | bytes 786440 | tf_op jit(solution)/shard_map/ppermute | solution.py:21
  105.9 39.5 %collective-permute-start.11 = (bf16[2,256,256]{1,2,0:T(8,128)(2,1)S(1)}, bf16[2,256,256]{1,2,0:T(8,128)(2,1)S(1)}, u32[]{:S(2)}, u32[]{:S(2)}) collective-permute-start(bf16[2,256,256]{1,2,0:T(8,128)(2,1)S(1)} %pad_maximum_fusion), channel_id=1, source_target_pairs={{0,11},{1,12},{2,13},{3,14},{4,15},{5,16},{6,17},{7,18},{8,19},{9,... | collective-permute-start | bytes 786440 | tf_op jit(solution)/shard_map/ppermute | solution.py:21
  125.0 32.0 %collective-permute-start.12 = (bf16[2,256,256]{1,2,0:T(8,128)(2,1)S(1)}, bf16[2,256,256]{1,2,0:T(8,128)(2,1)S(1)}, u32[]{:S(2)}, u32[]{:S(2)}) collective-permute-start(bf16[2,256,256]{1,2,0:T(8,128)(2,1)S(1)} %pad_maximum_fusion), channel_id=1, source_target_pairs={{0,12},{1,13},{2,14},{3,15},{4,16},{5,17},{6,18},{7,19},{8,20},{9,... | collective-permute-start | bytes 786440 | tf_op jit(solution)/shard_map/ppermute | solution.py:21
  128.2 33.0 %collective-permute-start.13 = (bf16[2,256,256]{1,2,0:T(8,128)(2,1)S(1)}, bf16[2,256,256]{1,2,0:T(8,128)(2,1)S(1)}, u32[]{:S(2)}, u32[]{:S(2)}) collective-permute-start(bf16[2,256,256]{1,2,0:T(8,128)(2,1)S(1)} %pad_maximum_fusion), channel_id=1, source_target_pairs={{0,13},{1,14},{2,15},{3,16},{4,17},{5,18},{6,19},{7,20},{8,21},{9,... | collective-permute-start | bytes 786440 | tf_op jit(solution)/shard_map/ppermute | solution.py:21
  132.5 45.8 %collective-permute-start.14 = (bf16[2,256,256]{1,2,0:T(8,128)(2,1)S(1)}, bf16[2,256,256]{1,2,0:T(8,128)(2,1)S(1)}, u32[]{:S(2)}, u32[]{:S(2)}) collective-permute-start(bf16[2,256,256]{1,2,0:T(8,128)(2,1)S(1)} %pad_maximum_fusion), channel_id=1, source_target_pairs={{0,14},{1,15},{2,16},{3,17},{4,18},{5,19},{6,20},{7,21},{8,22},{9,... | collective-permute-start | bytes 786440 | tf_op jit(solution)/shard_map/ppermute | solution.py:21
  134.9 57.9 %collective-permute-start.15 = (bf16[2,256,256]{1,2,0:T(8,128)(2,1)S(1)}, bf16[2,256,256]{1,2,0:T(8,128)(2,1)S(1)}, u32[]{:S(2)}, u32[]{:S(2)}) collective-permute-start(bf16[2,256,256]{1,2,0:T(8,128)(2,1)S(1)} %pad_maximum_fusion), channel_id=1, source_target_pairs={{0,15},{1,16},{2,17},{3,18},{4,19},{5,20},{6,21},{7,22},{8,23},{9,... | collective-permute-start | bytes 786440 | tf_op jit(solution)/shard_map/ppermute | solution.py:21
  145.4 52.9 %collective-permute-start.16 = (bf16[2,256,256]{1,2,0:T(8,128)(2,1)S(1)}, bf16[2,256,256]{1,2,0:T(8,128)(2,1)S(1)}, u32[]{:S(2)}, u32[]{:S(2)}) collective-permute-start(bf16[2,256,256]{1,2,0:T(8,128)(2,1)S(1)} %pad_maximum_fusion), channel_id=1, source_target_pairs={{0,16},{1,17},{2,18},{3,19},{4,20},{5,21},{6,22},{7,23},{8,24},{9,... | collective-permute-start | bytes 786440 | tf_op jit(solution)/shard_map/ppermute | solution.py:21
  210.0 2.3 copy-start.4
  210.0 3.2 copy-start.5
  218.9 0.7 copy-start.19
  218.9 0.9 copy-start.8
  219.0 147.7 %all-gather.2.cloned.1.call-start = ((), (), s32[]{:S(2)}) async-start(), calls=%async_computation.2 | async-start | bytes 6656000 | tf_op jit(solution)/shard_map/all_gather | solution.py:135
  219.9 3.2 copy-start.9
  223.1 140.7 %copy-start.11 = (f32[2560]{0:T(1024)S(1)}, f32[2560]{0:T(1024)}, u32[]{:S(2)}) copy-start(f32[2560]{0:T(1024)} %param.18) | copy-start | bytes 30724
  223.9 142.7 %copy-start.6 = (bf16[2,128,256]{2,1,0:T(8,128)(2,1)}, bf16[2,128,256]{2,1,0:T(8,128)(2,1)S(1)}, u32[]{:S(2)}) copy-start(bf16[2,128,256]{2,1,0:T(8,128)(2,1)S(1)} %scatter_fusion) | copy-start | bytes 393220
  361.7 2.5 copy-start.1
  366.6 4.2 %copy-start.2 = (f32[256,2560]{1,0:T(8,128)S(1)}, f32[256,2560]{1,0:T(8,128)}, u32[]{:S(2)}) copy-start(f32[256,2560]{1,0:T(8,128)} %all-reduce.2.cloned.1.call-done) | copy-start | bytes 7864324
  366.7 4.4 %copy-start.3 = (f32[256,2560]{1,0:T(8,128)S(1)}, f32[256,2560]{1,0:T(8,128)}, u32[]{:S(2)}) copy-start(f32[256,2560]{1,0:T(8,128)} %copy.26) | copy-start | bytes 7864324
  366.7 4.4 %copy-start.13 = (f32[2560]{0:T(1024)S(1)}, f32[2560]{0:T(1024)}, u32[]{:S(2)}) copy-start(f32[2560]{0:T(1024)} %param.19) | copy-start | bytes 30724
Sparse Core Ops, SparseCore 0:
  219.1 142.5 all-reduce.1
Sparse Core Ops, SparseCore 1:
  222.7 129.3 all-gather.1
